TPU v7x, 256 devices: a whole 4x4x8 slice. The times are simulated.
256 devices in a mesh: path: 64 (over z, x, core), rep: 4 (over y).
Axes of the slice: x: 4, y: 4, z: 8, core: 2. Of those that a mesh axis runs over, the one named last changes fastest.
Arguments:
- start_state: float32 [32, 65536], P(None, 'path'), may hold values from -1.8 to 1.8
- increments: float32 [2, 32, 65536], P(None, None, 'path'), may hold values from -6 to 6
- vol_factor: float32 [32, 32], replicated, may hold values from -0.3 to 0.3
- quad_dirs: float32 [223, 32], replicated, may hold values from -1.5 to 1.5
- bundle_ids: int32 [2, 65536, 1], P(None, 'path'), may hold values from 0 to 255; in each aligned block of 1024 rows (0 to 1023, 1024 to 2047, ..., all dimensions but the last counted through in order) at most 8 rows name the same one
- bundle_slot: int32 [256], replicated, may hold values from 0 to 255, each once
Outputs:
- values: float32 [2, 65536], P(None, 'path')
- coefficients: float32 [2, 256, 256], P(None, 'path', 'rep')
Inputs may be any that keep to these rules, and one draw needn't show every extreme that they name: `bundle_ids`: at each date, no bundle id appears more than 8 times among the paths of one device; in every draw some device holds exactly 8 paths of one bundle. A permutation: bundle b sits at slot bundle_slot[b], and slot s belongs to the owner s // 4 along path.
All inputs are finite; a program needn't handle non-finite values.
Results may differ from a plain program's by a relative error of at most 0.0003.
Values sent between devices are 32-bit elements; how exact they have to be, the bound alone decides.
No kernel may reach another device: no remote copies, remote signals or barrier semaphores. Data moves between devices by JAX's collectives and lax.ppermute only.
A program may use at most 64 MiB of HBM per device.

v0:
```python
import jax
import jax.numpy as jnp
from jax import lax
from jax.sharding import PartitionSpec as P

BASIS = 256


RIDGE_TERM = 32.0
DISCOUNT = 0.97
NOTIONAL = 10.0
HIGHEST = lax.Precision.HIGHEST


def basis_features(states, quad_dirs):
    projected = jnp.dot(quad_dirs, states, precision=HIGHEST, preferred_element_type=jnp.float32)
    constant = jnp.ones((1, states.shape[1]), jnp.float32)
    return jnp.concatenate([constant, states, projected * projected], axis=0)


def moment_features(states, quad_dirs, offsets):
    projected = jnp.dot(quad_dirs, states, precision=HIGHEST, preferred_element_type=jnp.float32)
    constant = jnp.ones((1, states.shape[1]), jnp.float32)
    return jnp.concatenate([constant, states, projected * projected + offsets[:, None]], axis=0)


def exercise_value(states):
    return NOTIONAL * jnp.maximum(jnp.mean(jnp.exp(states), axis=0) - 1.0, 0.0)


def backward_period(bundle_of, state_now, state_next, value_next, bundle_slot, quad_dirs, offsets):
    path_count = state_now.shape[1]
    bundles = bundle_slot.shape[0]
    owners = lax.axis_size("path")
    per_owner = bundles // owners
    capacity = max(2, 2 * path_count // bundles)
    column_count = BASIS // lax.axis_size("rep")
    rep_index = lax.axis_index("rep")
    share_count = 1
    share_slots = -(-capacity // share_count)
    padded_capacity = share_slots * share_count
    owner_block = per_owner * share_slots
    slot_of = jnp.take(bundle_slot, bundle_of)
    ranking = jnp.argsort(slot_of, stable=True)
    ordered = jnp.take(slot_of, ranking)
    group_start = jnp.searchsorted(ordered, ordered, side="left")
    rank_within = jnp.arange(path_count, dtype=jnp.int32) - group_start
    position = ordered * padded_capacity + rank_within
    regress_rows = jnp.concatenate(
        [basis_features(state_next, quad_dirs), value_next[None, :]], axis=0
    )
    row_count = regress_rows.shape[0]
    outgoing = jnp.zeros((row_count, bundles * padded_capacity), jnp.float32)
    outgoing = outgoing.at[:, position].set(jnp.take(regress_rows, ranking, axis=1))
    outgoing = outgoing.reshape(row_count, bundles, share_slots, share_count)
    outgoing = outgoing.reshape(row_count, owners, owner_block)
    arrived = lax.all_to_all(outgoing, "path", split_axis=1, concat_axis=1, tiled=True)
    arrived = arrived.reshape(row_count, owners * owner_block)
    features = arrived[:BASIS]
    target = arrived[BASIS]
    features = features.reshape(BASIS, owners, per_owner, share_slots)
    target = target.reshape(owners, per_owner, share_slots)
    column_block = lax.dynamic_slice_in_dim(features, rep_index * column_count, column_count, 0)
    gram_part = jnp.einsum("ksbm,csbm->bkc", features, column_block, precision=HIGHEST)
    gram_matrix = lax.all_gather(gram_part, "rep", axis=2, tiled=True)
    right_side = jnp.einsum("ksbm,sbm->bk", features, target, precision=HIGHEST)
    gram_matrix = gram_matrix + RIDGE_TERM * jnp.eye(BASIS, dtype=jnp.float32)
    factor = jnp.linalg.cholesky(gram_matrix)
    halfway = lax.linalg.triangular_solve(
        factor, right_side[:, :, None], left_side=True, lower=True
    )
    weights = lax.linalg.triangular_solve(
        factor, halfway, left_side=True, lower=True, transpose_a=True
    )[:, :, 0]
    weight_block = lax.dynamic_slice_in_dim(weights, rep_index * column_count, column_count, 1)
    weight_table = lax.all_gather(weight_block, "path", axis=0, tiled=True)
    picked = jnp.take(weight_table, slot_of, axis=0)
    moments = moment_features(state_now, quad_dirs, offsets)
    moment_block = lax.dynamic_slice_in_dim(moments, rep_index * column_count, column_count, 0)
    partial_terms = jnp.sum(picked.T * moment_block, axis=0)
    carried = lax.psum(partial_terms, "rep")
    value_now = jnp.maximum(exercise_value(state_now), DISCOUNT * carried)
    return (value_now, weight_block)


def body(start_state, increments, vol_factor, quad_dirs, bundle_ids, bundle_slot):
    middle = start_state + jnp.dot(
        vol_factor, increments[0], precision=HIGHEST, preferred_element_type=jnp.float32
    )
    final = middle + jnp.dot(
        vol_factor, increments[1], precision=HIGHEST, preferred_element_type=jnp.float32
    )
    mixed = jnp.dot(quad_dirs, vol_factor, precision=HIGHEST, preferred_element_type=jnp.float32)
    offsets = jnp.sum(mixed * mixed, axis=1)
    value_final = exercise_value(final)
    value_middle, weights_middle = backward_period(
        bundle_ids[0, :, 0], middle, final, value_final, bundle_slot, quad_dirs, offsets
    )
    value_start, weights_start = backward_period(
        bundle_ids[1, :, 0], start_state, middle, value_middle, bundle_slot, quad_dirs, offsets
    )
    return (jnp.stack([value_middle, value_start]), jnp.stack([weights_middle, weights_start]))


def solution(mesh):
    placed = (P(None, "path"), P(None, None, "path"), P(), P(), P(None, "path", None), P())
    return jax.shard_map(
        body,
        mesh=mesh,
        in_specs=placed,
        out_specs=(P(None, "path"), P(None, "path", "rep")),
        check_vma=False,
    )
```

profile of v0, /device:TPU:8, one launch (start us, length us, event | category | flops | bytes accessed | tf_op | source)
XLA Modules:
  0.0 985.1 jit_solution(9080812871805606301)
XLA Ops:
  7.9 6.9 gather_fusion.2
  15.4 4.4 sort.31
  19.8 4.5 gather_fusion.3
  24.3 50.7 %while.47 = (s32[]{:T(128)}, u32[1024]{0:T(1024)S(1)}, u32[1024]{0:T(1024)S(1)}, s32[1024]{0:T(1024)S(1)}, s32[]{:T(128)}, /*index=5*/s32[]{:T(128)}, s32[]{}) while((s32[]{:T(128)}, u32[1024]{0:T(1024)S(1)}, u32[1024]{0:T(1024)S(1)}, s32[1024]{0:T(1024)S(1)}, s32[]{:T(128)}, /*index=5*/s32[]{:T(128)}, s32[]{}) %tuple.133), condition=%wide.region_3.0_spmd.clone, body=%wide.region_2.5_spmd.clone.sunk | while | flops 19460 | bytes 67685 | solution.py:46
  24.4 4.5 gather_fusion
  29.0 4.5 gather_fusion
  33.6 4.5 gather_fusion
  38.2 4.5 gather_fusion
  42.8 4.5 gather_fusion
  47.4 4.5 gather_fusion
  52.0 4.5 gather_fusion
  56.7 4.5 gather_fusion
  61.3 4.5 gather_fusion
  65.9 4.5 gather_fusion
  70.5 4.5 gather_fusion
  75.1 6.9 gather_fusion.5
  82.6 4.4 sort.32
  87.5 4.5 gather_fusion.6
  92.7 50.7 %while.48 = (s32[]{:T(128)}, u32[1024]{0:T(1024)S(1)}, u32[1024]{0:T(1024)S(1)}, s32[1024]{0:T(1024)S(1)}, s32[]{:T(128)}, /*index=5*/s32[]{:T(128)}, s32[]{}) while((s32[]{:T(128)}, u32[1024]{0:T(1024)S(1)}, u32[1024]{0:T(1024)S(1)}, s32[1024]{0:T(1024)S(1)}, s32[]{:T(128)}, /*index=5*/s32[]{:T(128)}, s32[]{}) %tuple.130), condition=%wide.region_16.24_spmd.clone, body=%wide.region_15.23_spmd.clone.sunk | while | flops 19460 | bytes 67685 | solution.py:46
  92.7 4.5 gather_fusion.1
  97.3 4.5 gather_fusion.1
  101.9 4.5 gather_fusion.1
  106.5 4.5 gather_fusion.1
  111.1 4.5 gather_fusion.1
  115.7 4.5 gather_fusion.1
  120.3 4.5 gather_fusion.1
  124.9 4.5 gather_fusion.1
  129.6 4.5 gather_fusion.1
  134.2 4.5 gather_fusion.1
  138.8 4.5 gather_fusion.1
  146.8 10.5 %scatter_custom_fusion = f32[257,2048]{0,1:T(8,128)} fusion(s32[1024]{0:T(1024)S(1)} %get-tuple-element.286, f32[]{:T(128)} %constant.182.clone.1, f32[]{:T(128)} %constant.164.clone.2, pred[1024]{0:T(1024)(128)(4,1)S(1)} %get-tuple-element.260, f32[257,1024]{0,1:T(8,128)S(1)} %copy.82, s32[1024]{0:T(1024)S(1)} %fusion.64), kind=kCustom, calls=%fused_computation.30 | custom fusion | flops 263168 | bytes 3683336 | tf_op jit(solution)/shard_map/scatter | solution.py:54
  157.2 11.9 %all-to-all-start = ((f32[257,64,32]{0,2,1:T(8,128)}), f32[257,64,32]{0,2,1:T(8,128)S(1)}, u32[]{:S(2)}, u32[]{:S(2)}) async-start(f32[257,64,32]{0,2,1:T(8,128)} %bitcast.257), calls=%async_computation | async-start | bytes 6291456 | tf_op jit(solution)/shard_map/all_to_all | solution.py:57
  169.4 73.6 %all-to-all-done = f32[257,64,32]{0,2,1:T(8,128)S(1)} async-done(((f32[257,64,32]{0,2,1:T(8,128)}), f32[257,64,32]{0,2,1:T(8,128)S(1)}, u32[]{:S(2)}, u32[]{:S(2)}) %all-to-all-start) | async-done | bytes 2105376 | tf_op jit(solution)/shard_map/all_to_all | solution.py:57
  243.0 2.6 slice_bitcast_fusion.13
  245.6 3.8 copy.83
  249.4 5.1 fusion.13
  256.1 3.1 broadcast_add_fusion.2
  262.0 6.0 fusion.78
  268.6 7.8 all-gather.5.cloned.1.call-done
  279.2 47.3 %custom-call.25 = f32[4,128,128]{2,1,0:T(8,128)S(1)} custom-call(f32[4,128,128]{2,1,0:T(8,128)S(1)} %cholesky.198), custom_call_target="Cholesky" | custom-call | tf_op jit(solution)/shard_map/jit(cholesky)/cholesky | solution.py:68
  326.6 39.3 %custom-call.26 = f32[4,1,128,128]{2,3,1,0:T(8,128)S(1)} custom-call(f32[4,1,128,128]{3,2,1,0:T(8,128)S(1)} %select_bitcast_fusion.1), custom_call_target="InvertDiagBlocksLowerTriangular" | custom-call | tf_op jit(solution)/shard_map/jit(cholesky)/cholesky | solution.py:68
  367.1 46.9 %custom-call.27 = f32[4,128,128]{2,1,0:T(8,128)S(1)} custom-call(f32[4,128,128]{2,1,0:T(8,128)S(1)} %convolution_subtract_fusion.1), custom_call_target="Cholesky" | custom-call | tf_op jit(solution)/shard_map/jit(cholesky)/cholesky | solution.py:68
  414.6 4.2 while.49
  419.4 78.8 %custom-call.29 = f32[4,2,128,128]{2,3,1,0:T(8,128)S(1)} custom-call(f32[4,2,128,128]{3,2,1,0:T(8,128)S(1)} %bitcast.260), custom_call_target="InvertDiagBlocksLowerTriangular" | custom-call | tf_op jit(solution)/shard_map/triangular_solve/custom-call.4 | solution.py:72
  500.9 50.7 %all-gather = f32[256,64,1]{1,2,0:T(1,128)S(1)} all-gather(f32[4,64,1]{1,2,0:T(1,128)S(1)} %fusion.70), channel_id=2, replica_groups=mesh['path'=64,'rep'=4] {'path'}, dimensions={0}, use_global_device_ids=true | all-gather | bytes 66560 | tf_op jit(solution)/shard_map/all_gather | solution.py:76
  551.6 2.8 gather_fusion.4
  554.8 9.5 psum.14
  565.1 10.6 %scatter_custom_fusion.1 = f32[257,2048]{0,1:T(8,128)} fusion(s32[1024]{0:T(1024)} %get-tuple-element.285, f32[]{:T(128)} %constant.182.clone.1, f32[]{:T(128)} %constant.164.clone.2, pred[1024]{0:T(1024)(128)(4,1)S(1)} %copy-done.26, f32[257,1024]{0,1:T(8,128)S(1)} %copy.92, s32[1024]{0:T(1024)S(1)} %copy-done.14), kind=kCustom, calls=%fused_computation.28 | custom fusion | flops 263168 | bytes 3164160 | tf_op jit(solution)/shard_map/scatter | solution.py:54
  575.7 81.5 %all_to_all.10 = f32[257,64,32]{0,2,1:T(8,128)S(1)} all-to-all(f32[257,64,32]{0,2,1:T(8,128)} %bitcast.258), channel_id=1, replica_groups=mesh['path'=64,'rep'=4] {'path'}, dimensions={1} | all-to-all | bytes 4210688 | tf_op jit(solution)/shard_map/all_to_all | solution.py:57
  657.1 2.6 slice_bitcast_fusion.12
  659.7 3.8 copy.93
  663.5 5.1 fusion.16
  670.8 2.8 fusion.12
  674.6 1.8 copy.145
  676.5 6.0 fusion.79
  683.6 5.9 all-gather.7.cloned.1.call-done
  692.3 47.1 %custom-call.30 = f32[4,128,128]{2,1,0:T(8,128)S(1)} custom-call(f32[4,128,128]{2,1,0:T(8,128)S(1)} %cholesky.201), custom_call_target="Cholesky" | custom-call | tf_op jit(solution)/shard_map/jit(cholesky)/cholesky | solution.py:68
  739.6 39.3 %custom-call.31 = f32[4,1,128,128]{2,3,1,0:T(8,128)S(1)} custom-call(f32[4,1,128,128]{3,2,1,0:T(8,128)S(1)} %select_bitcast_fusion), custom_call_target="InvertDiagBlocksLowerTriangular" | custom-call | tf_op jit(solution)/shard_map/jit(cholesky)/cholesky | solution.py:68
  780.0 46.9 %custom-call.32 = f32[4,128,128]{2,1,0:T(8,128)S(1)} custom-call(f32[4,128,128]{2,1,0:T(8,128)S(1)} %convolution_subtract_fusion), custom_call_target="Cholesky" | custom-call | tf_op jit(solution)/shard_map/jit(cholesky)/cholesky | solution.py:68
  827.5 4.0 while.50
  831.6 78.9 %custom-call.34 = f32[4,2,128,128]{2,3,1,0:T(8,128)S(1)} custom-call(f32[4,2,128,128]{3,2,1,0:T(8,128)S(1)} %bitcast.259), custom_call_target="InvertDiagBlocksLowerTriangular" | custom-call | tf_op jit(solution)/shard_map/triangular_solve/custom-call.4 | solution.py:72
  913.2 50.7 %all-gather.1 = f32[256,64,1]{1,2,0:T(1,128)S(1)} all-gather(f32[4,64,1]{1,2,0:T(1,128)S(1)} %fusion.69), channel_id=3, replica_groups=mesh['path'=64,'rep'=4] {'path'}, dimensions={0}, use_global_device_ids=true | all-gather | bytes 66560 | tf_op jit(solution)/shard_map/all_gather | solution.py:76
  963.9 2.8 gather_fusion.7
  967.0 9.5 psum.15
  (264 shorter events, 42.5 us)
Async XLA Ops:
  7.2 137.4 %copy-start = (f32[223,32]{0,1:T(8,128)S(1)}, f32[223,32]{0,1:T(8,128)}, u32[]{:S(2)}) copy-start(f32[223,32]{0,1:T(8,128)} %param.26) | copy-start | bytes 85636
  7.2 0.8 copy-start.1
  86.9 0.6 copy-start.13
  92.6 50.7 %copy-start.9 = (f32[32,1024]{1,0:T(8,128)S(1)}, f32[32,1024]{1,0:T(8,128)}, u32[]{:S(2)}) copy-start(f32[32,1024]{1,0:T(8,128)} %param.23) | copy-start | bytes 393220
  92.6 50.7 %copy-start.11 = (f32[2,32,1024]{2,1,0:T(8,128)S(1)}, f32[2,32,1024]{2,1,0:T(8,128)}, u32[]{:S(2)}) copy-start(f32[2,32,1024]{2,1,0:T(8,128)} %param.24) | copy-start | bytes 786436
  92.7 50.7 %copy-start.12 = (f32[32,32]{1,0:T(8,128)S(1)}, f32[32,32]{1,0:T(8,128)}, u32[]{:S(2)}) copy-start(f32[32,32]{1,0:T(8,128)} %param.25) | copy-start | bytes 12292
  144.3 1.2 copy-start.7
  157.2 85.8 %all-to-all-start = ((f32[257,64,32]{0,2,1:T(8,128)}), f32[257,64,32]{0,2,1:T(8,128)S(1)}, u32[]{:S(2)}, u32[]{:S(2)}) async-start(f32[257,64,32]{0,2,1:T(8,128)} %bitcast.257), calls=%async_computation | async-start | bytes 6291456 | tf_op jit(solution)/shard_map/all_to_all | solution.py:57
  169.2 107.3 %all-gather.5.cloned.1.call-start = ((), (), s32[]{:S(2)}) async-start(), calls=%async_computation.2 | async-start | bytes 1310720 | tf_op jit(solution)/shard_map/all_gather | solution.py:65
  254.5 435.0 %all-gather.7.cloned.1.call-start = ((), (), s32[]{:S(2)}) async-start(), calls=%async_computation.3 | async-start | bytes 1310720 | tf_op jit(solution)/shard_map/all_gather | solution.py:65
  255.5 0.6 copy-start.24
  277.8 1.2 copy-start.2
  367.0 47.4 %copy-start.31 = (s32[2]{0:T(128)S(1)}, s32[2]{0:T(128)}, u32[]{:S(2)}) copy-start(s32[2]{0:T(128)} %iota_multiply_fusion) | copy-start | bytes 28
  414.5 83.6 %copy-start.23 = (f32[4,128,1]{1,0,2:T(4,128)S(1)}, f32[4,128,1]{1,0,2:T(4,128)}, u32[]{:S(2)}) copy-start(f32[4,128,1]{1,0,2:T(4,128)} %slice.172) | copy-start | bytes 6148
  418.8 0.6 copy-start.29
  500.9 50.7 %copy-start.15 = (f32[4,64,1]{1,2,0:T(1,128)}, f32[4,64,1]{1,2,0:T(1,128)S(1)}, u32[]{:S(2)}) copy-start(f32[4,64,1]{1,2,0:T(1,128)S(1)} %fusion.70) | copy-start | bytes 3076
  551.6 3.0 copy-start.5
  551.6 3.0 copy-start.8
  551.6 3.1 copy-start.28
  554.4 9.8 copy-start.17
  554.4 9.8 copy-start.4
  564.4 0.7 copy-start.14
  564.4 0.7 copy-start.26
  663.5 7.3 copy-start.25
  682.4 0.6 copy-start.19
  690.9 1.2 copy-start.3
  826.9 0.7 copy-start.30
  827.4 83.1 %copy-start.22 = (f32[4,128,1]{1,0,2:T(4,128)S(1)}, f32[4,128,1]{1,0,2:T(4,128)}, u32[]{:S(2)}) copy-start(f32[4,128,1]{1,0,2:T(4,128)} %slice.179) | copy-start | bytes 6148
  827.5 83.8 %copy-start.20 = (f32[4,1,256,1]{2,0,1,3:T(4,128)S(1)}, f32[4,1,256,1]{2,0,1,3:T(4,128)}, u32[]{:S(2)}) copy-start(f32[4,1,256,1]{2,0,1,3:T(4,128)} %copy-done.19) | copy-start | bytes 12292
  831.5 132.3 %copy-start.21 = (s32[1024]{0:T(1024)S(1)}, s32[1024]{0:T(1024)}, u32[]{:S(2)}) copy-start(s32[1024]{0:T(1024)} %fusion.68) | copy-start | bytes 12292
  963.8 3.0 copy-start.6
  963.8 3.0 copy-start.10
  963.9 3.1 copy-start.27
  966.7 9.8 copy-start.18
  966.7 10.4 %copy-start.16 = (f32[4,64,1]{1,2,0:T(1,128)S(1)}, f32[4,64,1]{1,2,0:T(1,128)}, u32[]{:S(2)}) copy-start(f32[4,64,1]{1,2,0:T(1,128)} %copy-done.15) | copy-start | bytes 3076
Sparse Core Ops, SparseCore 0:
  254.7 21.7 all-gather.4
  668.8 20.7 all-gather.6
where the time goes:
time: 994 us; the launch traced here: 985 us
  other arithmetic  466 us (47%)
  blocking collectives  202 us (20%)
  local copies, waits for them, and re-layouts  163 us (16%)
  waiting for transfers between devices  87.4 us (9%)
  matrix products  37.7 us (4%)
  between operations  15.3 us (2%)
  starting transfers between devices  12.2 us (1%)
    another operation x18, other arithmetic, backward_period(): factor = jnp.linalg.cholesky(gram_matrix)  268 us
    another operation x10, other arithmetic, backward_period(): lax.linalg.triangular_solve(factor, halfway, left_side=True, lower=True,...  159 us
    all_gather x2, blocking collectives, backward_period(): weight_table = lax.all_gather(weight_block, 'path', axis=0, tiled=True)  101 us
    gather x22, local copies, waits for them, and re-layouts, backward_period(): group_start = jnp.searchsorted(ordered, ordered, side='left')  99.6 us
    all_to_all x1, blocking collectives, backward_period(): lax.all_to_all(outgoing, 'path', split_axis=1, concat_axis=1, tiled=True)  81.5 us
    all_to_all x1, waiting for transfers between devices, backward_period(): lax.all_to_all(outgoing, 'path', split_axis=1, concat_axis=1, tiled=True)  73.6 us
    scatter x2, other arithmetic, backward_period(): outgoing.at[:, position].set(jnp.take(regress_rows, ranking, axis=1))  21 us
  transfers between devices with their start and end apart: 3, of which 3 were waited for; matrix products, arithmetic and copies ran while one was open for 3% of the time, Pallas kernels for 0%

commit v1 on v0

v1 whole, which is shorter than its diff:
```python
import jax
import jax.numpy as jnp
from jax import lax
from jax.sharding import PartitionSpec as P

BASIS = 256
MOST = 8

RIDGE_TERM = 32.0
DISCOUNT = 0.97
NOTIONAL = 10.0
HIGHEST = lax.Precision.HIGHEST


def exercise_value(states):
    return NOTIONAL * jnp.maximum(jnp.mean(jnp.exp(states), axis=0) - 1.0, 0.0)


def exercise_rows(states):
    return NOTIONAL * jnp.maximum(jnp.mean(jnp.exp(states), axis=1) - 1.0, 0.0)


def routing(bundle_of, bundle_slot, rep_index, reps):
    path_count = bundle_of.shape[0]
    bundles = bundle_slot.shape[0]
    labels = lax.broadcasted_iota(jnp.int32, (path_count, bundles), 1)
    slot_of = jnp.sum(jnp.where(bundle_of[:, None] == labels, bundle_slot[None, :], 0), axis=1)
    owners = bundles // reps
    later = lax.broadcasted_iota(jnp.int32, (path_count, path_count), 0)
    earlier = lax.broadcasted_iota(jnp.int32, (path_count, path_count), 1)
    same = (slot_of[:, None] == slot_of[None, :]) & (earlier < later)
    rank = jnp.sum(same.astype(jnp.int32), axis=1)
    mine = (slot_of % reps) == rep_index
    position = jnp.where(mine, (slot_of // reps) * MOST + rank, -1)
    places = lax.broadcasted_iota(jnp.int32, (owners * MOST, path_count), 0)
    return (places == position[None, :]).astype(jnp.float32)


def send_rows(onehot, rows):
    return lax.dot_general(onehot, rows, (((1,), (1,)), ((), ())), precision=HIGHEST,
                           preferred_element_type=jnp.float32)


def exchange(block, owners):
    shaped = block.reshape((owners, MOST) + block.shape[1:])
    arrived = lax.all_to_all(shaped, "path", 0, 0, tiled=True)
    return arrived.reshape(block.shape)


def features_of(present, states, quad_dirs):
    projected = lax.dot_general(states, quad_dirs, (((1,), (1,)), ((), ())), precision=HIGHEST,
                                preferred_element_type=jnp.float32)
    return jnp.concatenate([present, states, projected * projected], axis=1)


def moments_of(states, quad_dirs, offsets):
    projected = lax.dot_general(states, quad_dirs, (((1,), (1,)), ((), ())), precision=HIGHEST,
                                preferred_element_type=jnp.float32)
    constant = jnp.ones((states.shape[0], 1), jnp.float32)
    return jnp.concatenate([constant, states, projected * projected + offsets[None, :]], axis=1)


def factor_gram(features):
    gram = lax.dot_general(features, features, (((0,), (0,)), ((), ())), precision=HIGHEST,
                           preferred_element_type=jnp.float32)
    gram = gram + RIDGE_TERM * jnp.eye(BASIS, dtype=jnp.float32)
    return jnp.linalg.cholesky(gram)


def solve_weights(factor, features, values):
    right_side = lax.dot_general(features, values, (((0,), (0,)), ((), ())), precision=HIGHEST,
                                 preferred_element_type=jnp.float32)
    halfway = lax.linalg.triangular_solve(factor, right_side[:, None], left_side=True, lower=True)
    weights = lax.linalg.triangular_solve(factor, halfway, left_side=True, lower=True, transpose_a=True)
    return weights[:, 0]


def new_values(weights, current, quad_dirs, offsets):
    moments = moments_of(current, quad_dirs, offsets)
    carried = jnp.dot(moments, weights, precision=HIGHEST, preferred_element_type=jnp.float32)
    return jnp.maximum(exercise_rows(current), DISCOUNT * carried)


def go_home(onehot, owner_values, owners):
    back = exchange(owner_values, owners)
    local = jnp.dot(back, onehot, precision=HIGHEST, preferred_element_type=jnp.float32)
    return lax.psum(local, "rep")


def coefficient_block(weights, reps):
    shaped = weights.reshape(reps, BASIS // reps)
    return lax.all_to_all(shaped, "rep", 0, 0, tiled=True)


def body(start_state, increments, vol_factor, quad_dirs, bundle_ids, bundle_slot):
    reps = lax.axis_size("rep")
    owners = bundle_slot.shape[0] // reps
    rep_index = lax.axis_index("rep")
    middle = start_state + jnp.dot(
        vol_factor, increments[0], precision=HIGHEST, preferred_element_type=jnp.float32
    )
    final = middle + jnp.dot(
        vol_factor, increments[1], precision=HIGHEST, preferred_element_type=jnp.float32
    )
    mixed = jnp.dot(quad_dirs, vol_factor, precision=HIGHEST, preferred_element_type=jnp.float32)
    offsets = jnp.sum(mixed * mixed, axis=1)
    assets = start_state.shape[0]
    ones = jnp.ones((1, start_state.shape[1]), jnp.float32)

    late_map = routing(bundle_ids[0, :, 0], bundle_slot, rep_index, reps)
    early_map = routing(bundle_ids[1, :, 0], bundle_slot, rep_index, reps)

    late_rows = exchange(send_rows(late_map, jnp.concatenate([ones, middle, final], axis=0)), owners)
    early_rows = exchange(send_rows(early_map, jnp.concatenate([ones, start_state, middle], axis=0)), owners)

    present = late_rows[:, :1]
    current = late_rows[:, 1:1 + assets]
    following = late_rows[:, 1 + assets:]
    late_features = features_of(present, following, quad_dirs)
    late_factor = factor_gram(late_features)
    late_weights = solve_weights(late_factor, late_features, exercise_rows(following))
    late_owner_values = new_values(late_weights, current, quad_dirs, offsets)
    value_middle = go_home(late_map, late_owner_values, owners)

    present = early_rows[:, :1]
    current = early_rows[:, 1:1 + assets]
    following = early_rows[:, 1 + assets:]
    early_features = features_of(present, following, quad_dirs)
    early_factor = factor_gram(early_features)
    early_targets = exchange(send_rows(early_map, value_middle[None, :]), owners)[:, 0]
    early_weights = solve_weights(early_factor, early_features, early_targets)
    early_owner_values = new_values(early_weights, current, quad_dirs, offsets)
    value_start = go_home(early_map, early_owner_values, owners)

    coefficients = jnp.stack(
        [coefficient_block(late_weights, reps), coefficient_block(early_weights, reps)]
    )
    return (jnp.stack([value_middle, value_start]), coefficients)


def solution(mesh):
    placed = (P(None, "path"), P(None, None, "path"), P(), P(), P(None, "path", None), P())
    return jax.shard_map(
        body,
        mesh=mesh,
        in_specs=placed,
        out_specs=(P(None, "path"), P(None, "path", "rep")),
        check_vma=False,
    )
```

time: 994 us -> 266 us (0.27)
  other arithmetic: 466 us -> 114 us
  blocking collectives: 202 us -> 17.9 us
  local copies, waits for them, and re-layouts: 163 us -> 13.7 us
  waiting for transfers between devices: 87.4 us -> 34.2 us
  starting transfers between devices: 12.2 us -> 53.2 us
  matrix products: 37.7 us -> 23.9 us
  between operations: 15.3 us -> 3.8 us
    another operation x32 -> x21, other arithmetic: 428 us -> 109 us  [the longest x12 68.4 us: factor_gram(): return jnp.linalg.cholesky(gram)]
    gather x30 -> x0, local copies, waits for them, and re-layouts: 128 us -> none  [the longest x22 99.6 us: backward_period(): group_start = jnp.searchsorted(ordered, ordered, side='left')]
    all_gather x2 -> x0, blocking collectives: 101 us -> none  [backward_period(): weight_table = lax.all_gather(weight_block, 'path', axis=0, tiled=True)]
    all_to_all x1 -> x0, blocking collectives: 81.5 us -> none  [backward_period(): lax.all_to_all(outgoing, 'path', split_axis=1, concat_axis=1, tiled=True)]
    all_to_all x1 -> x7, starting transfers between devices: 11.9 us -> 53.2 us  [the longest x5 42.7 us: exchange(): arrived = lax.all_to_all(shaped, 'path', 0, 0, tiled=True)]
    all_to_all x1 -> x7, waiting for transfers between devices: 73.6 us -> 34.2 us  [the longest x5 31.1 us: exchange(): arrived = lax.all_to_all(shaped, 'path', 0, 0, tiled=True)]
    scatter x2 -> x0, other arithmetic: 21 us -> none  [backward_period(): outgoing.at[:, position].set(jnp.take(regress_rows, ranking, axis=1))]
    all_gather x2 -> x0, waiting for transfers between devices: 13.8 us -> none  [backward_period(): gram_matrix = lax.all_gather(gram_part, 'rep', axis=2, tiled=True)]
  transfers between devices with their start and end apart: 3 -> 7, of which waited for: 3 -> 4; matrix products, arithmetic and copies ran while one was open for 3% -> 26% of each run, Pallas kernels for 0% -> 0%
where the time goes in v1:
time: 266 us; the launch traced here: 261 us
  other arithmetic  114 us (43%)
  starting transfers between devices  53.2 us (20%)
  waiting for transfers between devices  34.2 us (13%)
  matrix products  23.9 us (9%)
  blocking collectives  17.9 us (7%)
  local copies, waits for them, and re-layouts  13.7 us (5%)
  between operations  3.8 us (1%)
    another operation x12, other arithmetic, factor_gram(): return jnp.linalg.cholesky(gram)  68.4 us
    all_to_all x5, starting transfers between devices, exchange(): arrived = lax.all_to_all(shaped, 'path', 0, 0, tiled=True)  42.7 us
    another operation x7, other arithmetic, solve_weights(): lax.linalg.triangular_solve(factor, halfway, left_side=True, lower=True,...  39.4 us
    all_to_all x5, waiting for transfers between devices, exchange(): arrived = lax.all_to_all(shaped, 'path', 0, 0, tiled=True)  31.1 us
    psum x2, blocking collectives, go_home(): return lax.psum(local, 'rep')  17.9 us
    dot_general x3, matrix products, send_rows(): lax.dot_general(onehot, rows, (((1,), (1,)), ((), ())), precision=HIGHEST...  11.4 us
    all_to_all x2, starting transfers between devices, coefficient_block(): return lax.all_to_all(shaped, 'rep', 0, 0, tiled=True)  10.5 us
    another operation x15, local copies, waits for them, and re-layouts, solve_weights(): lax.linalg.triangular_solve(factor, halfway, left_side=True, lower=True,...  8.04 us
  transfers between devices with their start and end apart: 7, of which 4 were waited for; matrix products, arithmetic and copies ran while one was open for 26% of the time, Pallas kernels for 0%

profile of v1, /device:TPU:8, one launch (start us, length us, event | category | flops | bytes accessed | tf_op | source)
XLA Modules:
  0.0 261.0 jit_solution(8161638728167208264)
XLA Ops:
  0.7 0.7 fusion.96
  1.4 1.6 select_reduce_fusion.1
  3.1 0.5 convert_reduce_fusion.1
  3.6 1.2 convolution_add_fusion.3
  5.1 1.9 fusion.10
  7.0 12.1 %all-to-all-start = ((f32[64,8,65]{2,1,0:T(8,128)}), f32[64,8,65]{2,1,0:T(8,128)S(1)}, u32[]{:S(2)}, u32[]{:S(2)}) async-start(f32[64,8,65]{2,1,0:T(8,128)} %fusion.10), calls=%async_computation | async-start | bytes 524288 | tf_op jit(solution)/shard_map/all_to_all | solution.py:46
  19.1 0.5 convert_reduce_fusion
  19.9 1.8 fusion.11
  21.7 10.2 %all-to-all-done = f32[64,8,65]{2,1,0:T(8,128)S(1)} async-done(((f32[64,8,65]{2,1,0:T(8,128)}), f32[64,8,65]{2,1,0:T(8,128)S(1)}, u32[]{:S(2)}, u32[]{:S(2)}) %all-to-all-start) | async-done | bytes 133152 | tf_op jit(solution)/shard_map/all_to_all | solution.py:46
  32.0 5.1 %all-to-all-start.2 = ((f32[64,8,65]{2,1,0:T(8,128)}), f32[64,8,65]{2,1,0:T(8,128)S(1)}, u32[]{:S(2)}, u32[]{:S(2)}) async-start(f32[64,8,65]{2,1,0:T(8,128)} %fusion.11), calls=%async_computation.2 | async-start | bytes 524288 | tf_op jit(solution)/shard_map/all_to_all | solution.py:46
  37.1 0.7 convolution_multiply_fusion.2
  38.0 11.8 %all-to-all-done.2 = f32[64,8,65]{2,1,0:T(8,128)S(1)} async-done(((f32[64,8,65]{2,1,0:T(8,128)}), f32[64,8,65]{2,1,0:T(8,128)S(1)}, u32[]{:S(2)}, u32[]{:S(2)}) %all-to-all-start.2) | async-done | bytes 133152 | tf_op jit(solution)/shard_map/all_to_all | solution.py:46
  50.0 0.7 convolution_multiply_fusion
  50.9 0.7 convolution_add_fusion.1
  51.8 11.7 %cholesky.130 = f32[128,128]{1,0:T(8,128)S(1)} custom-call(f32[128,128]{1,0:T(8,128)S(1)} %cholesky.194), custom_call_target="Cholesky" | custom-call | tf_op jit(solution)/shard_map/jit(cholesky)/cholesky | solution.py:67
  63.5 9.8 %custom-call.17 = f32[1,128,128]{1,2,0:T(8,128)S(1)} custom-call(f32[1,128,128]{2,1,0:T(8,128)S(1)} %get-tuple-element.66), custom_call_target="InvertDiagBlocksLowerTriangular" | custom-call | tf_op jit(solution)/shard_map/jit(cholesky)/cholesky | solution.py:67
  73.6 0.3 convolution_subtract_fusion.1
  73.9 12.1 %cholesky.147 = f32[128,128]{1,0:T(8,128)S(1)} custom-call(f32[128,128]{1,0:T(8,128)S(1)} %convolution_subtract_fusion.1), custom_call_target="Cholesky" | custom-call | tf_op jit(solution)/shard_map/jit(cholesky)/cholesky | solution.py:67
  86.0 0.7 compare_reduce_fusion.2
  88.1 4.1 %while.8 = (s32[]{:T(128)}, f32[256,256]{1,0:T(8,128)S(1)}, s32[2,2]{1,0:T(2,128)S(1)}, f32[2,128,128]{2,1,0:T(8,128)S(1)}, s32[]{:T(128)}) while((s32[]{:T(128)}, f32[256,256]{1,0:T(8,128)S(1)}, s32[2,2]{1,0:T(2,128)S(1)}, f32[2,128,128]{2,1,0:T(8,128)S(1)}, s32[]{:T(128)}) %tuple.63), condition=%wide.while_cond.1, body=%wide.while_body.1.sunk | while | flops 2 | bytes 131181 | solution.py:74
  88.1 0.7 fusion.126
  88.8 1.3 bitcast_dynamic-update-slice_fusion.4
  90.2 0.7 fusion.126
  90.8 1.3 bitcast_dynamic-update-slice_fusion.4
  92.2 19.7 %custom-call.19 = f32[2,128,128]{1,2,0:T(8,128)S(1)} custom-call(f32[2,128,128]{2,1,0:T(8,128)S(1)} %get-tuple-element.34), custom_call_target="InvertDiagBlocksLowerTriangular" | custom-call | tf_op jit(solution)/shard_map/triangular_solve/custom-call.4 | solution.py:74
  111.9 0.5 convolution_bitcast_fusion.1
  113.7 0.7 fusion.8
  114.4 0.5 fusion.26
  114.9 0.7 all_to_all.34
  115.6 5.0 %all-to-all-start.1 = ((f32[64,1,8]{2,1,0:T(1,128)}), f32[64,1,8]{2,1,0:T(1,128)S(1)}, u32[]{:S(2)}, u32[]{:S(2)}) async-start(f32[64,1,8]{2,1,0:T(1,128)} %bitcast.36), calls=%async_computation.1 | async-start | bytes 65536 | tf_op jit(solution)/shard_map/all_to_all | solution.py:46
  120.8 0.7 convolution_add_fusion
  121.6 11.7 %cholesky.164 = f32[128,128]{1,0:T(8,128)S(1)} custom-call(f32[128,128]{1,0:T(8,128)S(1)} %cholesky.197), custom_call_target="Cholesky" | custom-call | tf_op jit(solution)/shard_map/jit(cholesky)/cholesky | solution.py:67
  133.4 9.8 %custom-call.20 = f32[1,128,128]{1,2,0:T(8,128)S(1)} custom-call(f32[1,128,128]{2,1,0:T(8,128)S(1)} %get-tuple-element.70), custom_call_target="InvertDiagBlocksLowerTriangular" | custom-call | tf_op jit(solution)/shard_map/jit(cholesky)/cholesky | solution.py:67
  143.7 11.7 %cholesky.181 = f32[128,128]{1,0:T(8,128)S(1)} custom-call(f32[128,128]{1,0:T(8,128)S(1)} %convolution_subtract_fusion), custom_call_target="Cholesky" | custom-call | tf_op jit(solution)/shard_map/jit(cholesky)/cholesky | solution.py:67
  155.5 0.7 compare_reduce_fusion
  157.5 4.2 %while.9 = (s32[]{:T(128)}, f32[256,256]{1,0:T(8,128)S(1)}, s32[2,2]{1,0:T(2,128)S(1)}, f32[2,128,128]{2,1,0:T(8,128)S(1)}, s32[]{:T(128)}) while((s32[]{:T(128)}, f32[256,256]{1,0:T(8,128)S(1)}, s32[2,2]{1,0:T(2,128)S(1)}, f32[2,128,128]{2,1,0:T(8,128)S(1)}, s32[]{:T(128)}) %tuple.66), condition=%wide.while_cond.1.clone, body=%wide.while_body.1.clone.sunk | while | flops 2 | bytes 131181 | solution.py:74
  157.5 0.6 fusion.127
  158.1 1.4 bitcast_dynamic-update-slice_fusion.5
  159.5 0.6 fusion.127
  160.1 1.4 bitcast_dynamic-update-slice_fusion.5
  161.6 0.7 fusion.9
  162.4 0.5 broadcast.389
  163.0 0.7 reduce.25
  163.8 0.7 fusion.4
  164.5 8.7 %psum.14 = f32[1024]{0:T(1024)S(1)} all-reduce(f32[1024]{0:T(1024)S(1)} %bitcast.213), channel_id=1, replica_groups=mesh['path'=64,'rep'=4] {'rep'}, use_global_device_ids=true, to_apply=%region_9.13 | all-reduce | flops 1024 | bytes 8192 | tf_op jit(solution)/shard_map/psum | solution.py:87
  173.2 7.7 %fusion.12 = f32[64,8,1]{1,2,0:T(1,128)} fusion(f32[1024,1,1]{0,1,2:T(1,128)S(1)} %bitcast.207, s32[1024]{0:T(1024)S(1)} %fusion.71, s32[64,8]{1,0:T(8,128)S(1)} %multiply_add_fusion), kind=kOutput, calls=%fused_computation.32 | convolution fusion | flops 6815744 | bytes 12288 | tf_op jit(solution)/shard_map/dot_general | solution.py:40
  180.9 10.3 %all-to-all-start.3 = ((f32[64,8,1]{1,2,0:T(1,128)}), f32[64,8,1]{1,2,0:T(1,128)S(1)}, u32[]{:S(2)}, u32[]{:S(2)}) async-start(f32[64,8,1]{1,2,0:T(1,128)} %fusion.12), calls=%async_computation.3 | async-start | bytes 65536 | tf_op jit(solution)/shard_map/all_to_all | solution.py:46
  191.2 0.7 all_to_all.40
  191.9 19.7 %custom-call.22 = f32[2,128,128]{1,2,0:T(8,128)S(1)} custom-call(f32[2,128,128]{2,1,0:T(8,128)S(1)} %get-tuple-element.36), custom_call_target="InvertDiagBlocksLowerTriangular" | custom-call | tf_op jit(solution)/shard_map/triangular_solve/custom-call.4 | solution.py:74
  211.6 5.7 %all-to-all-start.5 = ((f32[4,1,64]{2,1,0:T(1,128)}), f32[4,1,64]{2,1,0:T(1,128)S(1)}, u32[]{:S(2)}, u32[]{:S(2)}) async-start(f32[4,1,64]{2,1,0:T(1,128)} %bitcast.78), calls=%async_computation.5 | async-start | bytes 4096 | tf_op jit(solution)/shard_map/all_to_all | solution.py:92
  217.3 0.7 reduce.26
  218.1 0.5 convolution_bitcast_fusion
  219.8 0.5 fusion.31
  220.3 0.7 all_to_all.42
  221.0 4.8 %all-to-all-start.6 = ((f32[4,1,64]{2,1,0:T(1,128)}), f32[4,1,64]{2,1,0:T(1,128)S(1)}, u32[]{:S(2)}, u32[]{:S(2)}) async-start(f32[4,1,64]{2,1,0:T(1,128)} %bitcast.80), calls=%async_computation.6 | async-start | bytes 4096 | tf_op jit(solution)/shard_map/all_to_all | solution.py:92
  225.8 0.7 all_to_all.38
  226.5 3.1 %all-to-all-done.6 = f32[4,1,64]{2,1,0:T(1,128)S(1)} async-done(((f32[4,1,64]{2,1,0:T(1,128)}), f32[4,1,64]{2,1,0:T(1,128)S(1)}, u32[]{:S(2)}, u32[]{:S(2)}) %all-to-all-start.6) | async-done | bytes 1056 | tf_op jit(solution)/shard_map/all_to_all | solution.py:92
  229.5 10.3 %all-to-all-start.4 = ((f32[64,1,8]{2,1,0:T(1,128)}), f32[64,1,8]{2,1,0:T(1,128)S(1)}, u32[]{:S(2)}, u32[]{:S(2)}) async-start(f32[64,1,8]{2,1,0:T(1,128)} %bitcast.76), calls=%async_computation.4 | async-start | bytes 65536 | tf_op jit(solution)/shard_map/all_to_all | solution.py:46
  239.8 0.6 pad_maximum_fusion.7
  240.4 9.0 %all-to-all-done.4 = f32[64,1,8]{2,1,0:T(1,128)S(1)} async-done(((f32[64,1,8]{2,1,0:T(1,128)}), f32[64,1,8]{2,1,0:T(1,128)S(1)}, u32[]{:S(2)}, u32[]{:S(2)}) %all-to-all-start.4) | async-done | bytes 2080 | tf_op jit(solution)/shard_map/all_to_all | solution.py:46
  249.4 0.7 reduce.27
  250.3 0.7 fusion.2
  251.0 9.2 %psum.15 = f32[1,1024]{1,0:T(1,128)S(1)} all-reduce(f32[1,1024]{1,0:T(1,128)S(1)} %fusion.2), channel_id=1, replica_groups=mesh['path'=64,'rep'=4] {'rep'}, use_global_device_ids=true, to_apply=%region_13.17 | all-reduce | flops 1024 | bytes 8192 | tf_op jit(solution)/shard_map/psum | solution.py:87
  260.2 0.6 pad_maximum_fusion.6
  (74 shorter events, 5.8 us)
Async XLA Ops:
  0.6 19.0 %copy-start = (f32[223,32]{0,1:T(8,128)S(1)}, f32[223,32]{0,1:T(8,128)}, u32[]{:S(2)}) copy-start(f32[223,32]{0,1:T(8,128)} %param.14) | copy-start | bytes 85636
  0.6 4.2 %copy-start.1 = (f32[2,32,1024]{2,1,0:T(8,128)S(1)}, f32[2,32,1024]{2,1,0:T(8,128)}, u32[]{:S(2)}) copy-start(f32[2,32,1024]{2,1,0:T(8,128)} %param.12) | copy-start | bytes 786436
  0.7 4.2 %copy-start.3 = (f32[32,32]{1,0:T(8,128)S(1)}, f32[32,32]{1,0:T(8,128)}, u32[]{:S(2)}) copy-start(f32[32,32]{1,0:T(8,128)} %param.13) | copy-start | bytes 12292
  7.0 12.9 %copy-start.2 = (f32[32,1024]{1,0:T(8,128)S(1)}, f32[32,1024]{1,0:T(8,128)}, u32[]{:S(2)}) copy-start(f32[32,1024]{1,0:T(8,128)} %param.11) | copy-start | bytes 393220
  7.0 25.0 %all-to-all-start = ((f32[64,8,65]{2,1,0:T(8,128)}), f32[64,8,65]{2,1,0:T(8,128)S(1)}, u32[]{:S(2)}, u32[]{:S(2)}) async-start(f32[64,8,65]{2,1,0:T(8,128)} %fusion.10), calls=%async_computation | async-start | bytes 524288 | tf_op jit(solution)/shard_map/all_to_all | solution.py:46
  32.0 17.9 %all-to-all-start.2 = ((f32[64,8,65]{2,1,0:T(8,128)}), f32[64,8,65]{2,1,0:T(8,128)S(1)}, u32[]{:S(2)}, u32[]{:S(2)}) async-start(f32[64,8,65]{2,1,0:T(8,128)} %fusion.11), calls=%async_computation.2 | async-start | bytes 524288 | tf_op jit(solution)/shard_map/all_to_all | solution.py:46
  115.6 46.8 %all-to-all-start.1 = ((f32[64,1,8]{2,1,0:T(1,128)}), f32[64,1,8]{2,1,0:T(1,128)S(1)}, u32[]{:S(2)}, u32[]{:S(2)}) async-start(f32[64,1,8]{2,1,0:T(1,128)} %bitcast.36), calls=%async_computation.1 | async-start | bytes 65536 | tf_op jit(solution)/shard_map/all_to_all | solution.py:46
  180.9 30.7 %all-to-all-start.3 = ((f32[64,8,1]{1,2,0:T(1,128)}), f32[64,8,1]{1,2,0:T(1,128)S(1)}, u32[]{:S(2)}, u32[]{:S(2)}) async-start(f32[64,8,1]{1,2,0:T(1,128)} %fusion.12), calls=%async_computation.3 | async-start | bytes 65536 | tf_op jit(solution)/shard_map/all_to_all | solution.py:46
  211.6 9.5 %all-to-all-start.5 = ((f32[4,1,64]{2,1,0:T(1,128)}), f32[4,1,64]{2,1,0:T(1,128)S(1)}, u32[]{:S(2)}, u32[]{:S(2)}) async-start(f32[4,1,64]{2,1,0:T(1,128)} %bitcast.78), calls=%async_computation.5 | async-start | bytes 4096 | tf_op jit(solution)/shard_map/all_to_all | solution.py:92
  221.0 8.5 %all-to-all-start.6 = ((f32[4,1,64]{2,1,0:T(1,128)}), f32[4,1,64]{2,1,0:T(1,128)S(1)}, u32[]{:S(2)}, u32[]{:S(2)}) async-start(f32[4,1,64]{2,1,0:T(1,128)} %bitcast.80), calls=%async_computation.6 | async-start | bytes 4096 | tf_op jit(solution)/shard_map/all_to_all | solution.py:92
  229.5 19.9 %all-to-all-start.4 = ((f32[64,1,8]{2,1,0:T(1,128)}), f32[64,1,8]{2,1,0:T(1,128)S(1)}, u32[]{:S(2)}, u32[]{:S(2)}) async-start(f32[64,1,8]{2,1,0:T(1,128)} %bitcast.76), calls=%async_computation.4 | async-start | bytes 65536 | tf_op jit(solution)/shard_map/all_to_all | solution.py:46
